TPU v7x, 256 devices: a whole 4x4x8 slice. The times are simulated.
256 devices in a mesh: ctx: 16 (over x, z_hi, core), exp: 16 (over z_lo, y).
Axes of the slice: x: 4, y: 4, z: 8 (z_hi: 2, z_lo: 4; z = z_hi * 4 + z_lo), core: 2. Of those that a mesh axis runs over, the one named last changes fastest.
Arguments:
- queries: bfloat16 [16, 1024, 2560], P('exp', 'ctx'), may hold values from -4.5 to 4.5
- keys: bfloat16 [16, 1024, 512], P('exp', 'ctx'), may hold values from -4.5 to 4.5
- values: bfloat16 [16, 1024, 512], P('exp', 'ctx'), may hold values from -6 to 6
- doc_lengths: int32 [16, 4], P('exp'), may hold values from 1 to 512, 1024 in all within a row
- resid: bfloat16 [16, 1024, 5120], P('exp', 'ctx'), may hold values from -6 to 6
- out_weight: bfloat16 [2560, 5120], P(('ctx', 'exp')), may hold values from -1 to 1
- norm_gain: bfloat16 [5120], replicated, may hold values from 0.099609375 to 1.8984375
- router_weight: bfloat16 [5120, 16], replicated, may hold values from -0.078125 to 0.078125
- expert_ids: int32 [16, 1024, 1], P('exp', 'ctx'), may hold values from 0 to 15; in each aligned block of 64 rows (0 to 63, 64 to 127, ..., all dimensions but the last counted through in order) at most 5 rows name the same one
- gate_weight: bfloat16 [16, 5120, 4096], P('exp', None, 'ctx'), may hold values from -0.078125 to 0.078125
- up_weight: bfloat16 [16, 5120, 4096], P('exp', None, 'ctx'), may hold values from -0.078125 to 0.078125
- down_weight: bfloat16 [16, 4096, 5120], P('exp', 'ctx'), may hold values from -0.375 to 0.375
Outputs:
- layer_out: bfloat16 [16, 1024, 5120], P('exp', 'ctx')
Inputs may be any that keep to these rules, and one draw needn't show every extreme that they name: `expert_ids`: among the 64 positions p = c * 64 .. c * 64 + 63 of one sequence, for any c, no expert is named more than 5 times.
All inputs are finite; a program needn't handle non-finite values.
Results may differ from a plain program's by a relative error of at most 0.017.
Values may be sent and summed in bfloat16 or wider, within the bound.
No kernel may reach another device: no remote copies, remote signals or barrier semaphores. Data moves between devices by JAX's collectives and lax.ppermute only.
A program may use at most 128 MiB of HBM per device.

v0:
```python
import math
import jax
import jax.numpy as jnp
from jax import lax
from jax.sharding import PartitionSpec as P

HEAD_SIZE = 128


def doc_number(positions, bounds):
    return jnp.sum((positions[:, None] >= bounds[None, :]).astype(jnp.int32), axis=1)


def local(
    queries,
    keys,
    values,
    doc_lengths,
    resid,
    out_weight,
    norm_gain,
    router_weight,
    expert_ids,
    gate_weight,
    up_weight,
    down_weight,
):
    tok_rows = queries.shape[1]
    width = resid.shape[2]
    n_ctx = lax.axis_size("ctx")
    n_exp = lax.axis_size("exp")
    positions = lax.axis_index("ctx") * tok_rows + jnp.arange(tok_rows, dtype=jnp.int32)
    bounds = jnp.cumsum(doc_lengths[0])
    query_doc = doc_number(positions, bounds)
    kv_heads = keys.shape[2] // HEAD_SIZE
    head_groups = queries.shape[2] // keys.shape[2]
    heads_of_query = queries[0].reshape(tok_rows, kv_heads, head_groups, HEAD_SIZE)
    scale = 1.0 / math.sqrt(HEAD_SIZE)
    best = jnp.full((kv_heads, head_groups, tok_rows), -1e30, jnp.float32)
    key_piece = lax.all_gather(keys[0], "ctx", axis=0, tiled=True)
    value_piece = lax.all_gather(values[0], "ctx", axis=0, tiled=True)
    count = key_piece.shape[0]
    heads_of_key = key_piece.reshape(count, kv_heads, HEAD_SIZE)
    heads_of_value = value_piece.reshape(count, kv_heads, HEAD_SIZE)
    scores = (
        jnp.einsum(
            "tkgd,nkd->kgtn", heads_of_query, heads_of_key, preferred_element_type=jnp.float32
        )
        * scale
    )
    key_pos = jnp.arange(count, dtype=jnp.int32)
    visible = (key_pos[None, :] <= positions[:, None]) & (
        doc_number(key_pos, bounds)[None, :] == query_doc[:, None]
    )
    masked = jnp.where(visible, scores, -1e30)
    newbest = jnp.maximum(best, jnp.max(masked, axis=-1))
    weights = jnp.where(visible, jnp.exp(masked - newbest[..., None]), 0.0)
    total = jnp.sum(weights, axis=-1)
    accum = jnp.einsum(
        "kgtn,nkd->kgtd",
        weights.astype(jnp.bfloat16),
        heads_of_value,
        preferred_element_type=jnp.float32,
    )
    best, total, accum = (newbest, total, accum)
    attended = (
        (accum / total[..., None]).transpose(2, 0, 1, 3).reshape(tok_rows, -1).astype(jnp.bfloat16)
    )
    qwidth = attended.shape[1]
    proj_rows = lax.all_gather(out_weight, "exp", axis=0, tiled=True)
    feature_block = lax.all_to_all(
        attended.reshape(tok_rows, n_ctx, qwidth // n_ctx),
        "ctx",
        split_axis=1,
        concat_axis=0,
        tiled=True,
    )
    feature_rows = feature_block.reshape(n_ctx * tok_rows, -1)
    attn_sum = lax.psum_scatter(
        jnp.dot(feature_rows, proj_rows, preferred_element_type=jnp.float32).astype(jnp.bfloat16),
        "ctx",
        scatter_dimension=0,
        tiled=True,
    )
    hidden_state = resid[0].astype(jnp.float32) + attn_sum.astype(jnp.float32)
    mean_square = jnp.mean(hidden_state * hidden_state, axis=-1, keepdims=True)
    normed = hidden_state * lax.rsqrt(mean_square + 1e-05) * norm_gain.astype(jnp.float32)
    normed_b = normed.astype(jnp.bfloat16)
    logits = jnp.dot(normed_b, router_weight, preferred_element_type=jnp.float32)
    n_experts = router_weight.shape[1]
    chosen = expert_ids[0, :, 0]
    picked = chosen[:, None] == jnp.arange(n_experts, dtype=jnp.int32)[None, :]
    score = jax.nn.sigmoid(jnp.sum(jnp.where(picked, logits, 0.0), axis=-1))
    routed = (normed * score[:, None]).astype(jnp.bfloat16)
    capacity = max(2, tok_rows // n_experts + tok_rows // (4 * n_experts))
    lower = jnp.tril(jnp.ones((tok_rows, tok_rows), jnp.float32), -1)
    earlier = jnp.dot(lower, picked.astype(jnp.float32), preferred_element_type=jnp.float32)
    slot_rank = jnp.sum(jnp.where(picked, earlier, 0.0), axis=-1).astype(jnp.int32)
    selector = picked[:, :, None] & (
        slot_rank[:, None, None] == jnp.arange(capacity, dtype=jnp.int32)[None, None, :]
    )
    selector_b = selector.astype(jnp.bfloat16)
    outgoing = jnp.einsum(
        "tes,td->esd", selector_b, routed, preferred_element_type=jnp.float32
    ).astype(jnp.bfloat16)
    arrived = lax.all_to_all(outgoing, "exp", split_axis=0, concat_axis=0, tiled=True)
    arrived_rows = arrived.reshape(-1, width)
    gate_local = gate_weight[0]
    up_local = up_weight[0]
    down_local = down_weight[0]
    piece = lax.all_gather(arrived_rows, "ctx", axis=0, tiled=True)
    gate = jnp.dot(piece, gate_local, preferred_element_type=jnp.float32)
    up = jnp.dot(piece, up_local, preferred_element_type=jnp.float32)
    inner = (jax.nn.silu(gate) * up).astype(jnp.bfloat16)
    summed = lax.psum_scatter(
        jnp.dot(inner, down_local, preferred_element_type=jnp.float32).astype(jnp.bfloat16),
        "ctx",
        scatter_dimension=0,
        tiled=True,
    )
    expert_out = summed.reshape(n_exp, capacity, width)
    returned = lax.all_to_all(expert_out, "exp", split_axis=0, concat_axis=0, tiled=True)
    combined = jnp.einsum("tes,esd->td", selector_b, returned, preferred_element_type=jnp.float32)
    layer_out = (hidden_state + combined).astype(jnp.bfloat16)
    return layer_out[None]


def solution(mesh):
    in_specs = (
        P("exp", "ctx", None),
        P("exp", "ctx", None),
        P("exp", "ctx", None),
        P("exp", None),
        P("exp", "ctx", None),
        P(("ctx", "exp"), None),
        P(),
        P(),
        P("exp", "ctx", None),
        P("exp", None, "ctx"),
        P("exp", None, "ctx"),
        P("exp", "ctx", None),
    )
    out_specs = P("exp", "ctx", None)
    return jax.shard_map(local, mesh=mesh, in_specs=in_specs, out_specs=out_specs, check_vma=False)
```

profile of v0, /device:TPU:32, one launch (start us, length us, event | category | flops | bytes accessed | tf_op | source)
XLA Modules:
  0.0 811.9 jit_solution(17532757584282745511)
XLA Ops:
  6.5 0.0 all-gather.10.cloned.1.call-start
  6.5 0.7 all-gather.10.cloned.1.call-update
  7.3 0.0 all-gather.12.cloned.1.call-start
  7.3 0.7 all-gather.12.cloned.1.call-update
  8.0 0.0 all-gather.14.cloned.1.call-start
  8.1 0.7 all-gather.14.cloned.1.call-update
  8.7 1.4 reshape_squeeze.3
  10.1 0.8 reduce-window.8
  11.0 0.1 convert_reduce_fusion
  11.0 0.1 convert_reduce_fusion.1
  11.1 0.1 fusion.49
  11.3 56.0 %all-gather.10.cloned.1.call-done = bf16[1,1024,512]{2,1,0:T(8,128)(2,1)} async-done(((bf16[1,64,512]{2,1,0:T(8,128)(2,1)}), bf16[1,1024,512]{2,1,0:T(8,128)(2,1)}) %all-gather.10.cloned.1.call-update) | async-done | bytes 1048592 | tf_op jit(solution)/shard_map/all_gather | solution.py:40
  67.2 2.3 copy.34
  69.5 51.5 %all-gather.12.cloned.1.call-done = bf16[1,1024,512]{2,1,0:T(8,128)(2,1)} async-done(((bf16[1,64,512]{2,1,0:T(8,128)(2,1)}), bf16[1,1024,512]{2,1,0:T(8,128)(2,1)}) %all-gather.12.cloned.1.call-update) | async-done | bytes 1048592 | tf_op jit(solution)/shard_map/all_gather | solution.py:41
  121.1 2.3 copy.37
  123.3 2.4 fusion.3
  125.7 1.6 fusion.4
  127.4 1.5 fusion.32
  128.9 0.2 copy.39
  129.1 1.4 convert_element_type.64
  130.5 2.0 copy.40
  132.5 4.2 all-to-all-start
  136.8 0.0 reduce-scatter.3.cloned.1.call-start
  136.8 66.1 %all-gather.14.cloned.1.call-done = bf16[16,10,5120]{2,1,0:T(8,128)(2,1)} async-done(((bf16[1,10,5120]{2,1,0:T(8,128)(2,1)}), bf16[16,10,5120]{2,1,0:T(8,128)(2,1)}) %all-gather.14.cloned.1.call-update) | async-done | bytes 1638416 | tf_op jit(solution)/shard_map/all_gather | solution.py:70
  202.9 4.0 reshape.133
  207.0 0.0 all-to-all-done
  207.0 6.9 convolution_convert_fusion.1
  213.9 0.0 reduce-scatter.3.cloned.1.call-update
  214.0 0.0 all-gather.8.cloned.1.call-start
  214.0 0.6 copy-done.6
  214.6 0.2 fusion.28
  214.9 159.8 %reduce-scatter.3.cloned.1.call-done = bf16[64,5120]{1,0:T(8,128)(2,1)} async-done(((bf16[1024,5120]{1,0:T(8,128)(2,1)}), bf16[64,5120]{1,0:T(8,128)(2,1)}) %reduce-scatter.3.cloned.1.call-update) | async-done | bytes 655376 | tf_op jit(solution)/shard_map/reduce_scatter | solution.py:79
  374.7 1.5 multiply_reduce_fusion
  376.2 1.5 fusion.27
  377.7 0.5 convolution_convert_fusion.2
  378.1 0.5 copy.42
  378.6 36.6 %all_to_all.25 = bf16[16,5,5120]{2,1,0:T(8,128)(2,1)} all-to-all(bf16[16,5,5120]{2,1,0:T(8,128)(2,1)S(1)} %copy.42), channel_id=1, replica_groups=mesh['ctx'=16,'exp'=16] {'exp'}, dimensions={0} | all-to-all | bytes 1638400 | tf_op jit(solution)/shard_map/all_to_all | solution.py:106
  415.2 2.2 reshape.125
  417.4 0.0 all-gather.8.cloned.1.call-update
  417.5 0.2 reduce-scatter.5.cloned.1.call-start
  417.7 139.5 %all-gather.8.cloned.1.call-done = bf16[1280,5120]{1,0:T(8,128)(2,1)} async-done(((bf16[80,5120]{1,0:T(8,128)(2,1)}), bf16[1280,5120]{1,0:T(8,128)(2,1)}) %all-gather.8.cloned.1.call-update) | async-done | bytes 13107216 | tf_op jit(solution)/shard_map/all_gather | solution.py:111
  557.2 10.1 %fusion.8 = f32[1280,256]{1,0:T(8,128)} fusion(bf16[1280,5120]{1,0:T(8,128)(2,1)} %all-gather.8.cloned.1.call-done, bf16[1,5120,256]{2,1,0:T(8,128)(2,1)} %param.21), kind=kOutput, calls=%fused_computation.15 | convolution fusion | flops 3355443200 | bytes 17039360 | tf_op jit(solution)/shard_map/dot_general | solution.py:112
  567.3 20.4 %convolution_convert_fusion = bf16[1280,5120]{1,0:T(8,128)(2,1)} fusion(bf16[1,256,5120]{2,1,0:T(8,128)(2,1)S(1)} %copy-done, bf16[1280,5120]{1,0:T(8,128)(2,1)} %all-gather.8.cloned.1.call-done, bf16[1,5120,256]{2,1,0:T(8,128)(2,1)} %param.22, f32[1280,256]{1,0:T(8,128)} %fusion.8), kind=kOutput, calls=%fused_computation | convolution fusion | flops 6719406080 | bytes 32768000 | tf_op jit(solution)/shard_map/dot_general | solution.py:116
  587.7 0.0 reduce-scatter.5.cloned.1.call-update
  587.7 176.1 %reduce-scatter.5.cloned.1.call-done = bf16[80,5120]{1,0:T(8,128)(2,1)} async-done(((bf16[1280,5120]{1,0:T(8,128)(2,1)}), bf16[80,5120]{1,0:T(8,128)(2,1)}) %reduce-scatter.5.cloned.1.call-update) | async-done | bytes 819216 | tf_op jit(solution)/shard_map/reduce_scatter | solution.py:115
  763.7 2.2 reshape.126
  766.0 37.4 %all_to_all.26 = bf16[16,5,5120]{2,1,0:T(8,128)(2,1)S(1)} all-to-all(bf16[16,5,5120]{2,1,0:T(8,128)(2,1)} %reshape.126), channel_id=1, replica_groups=mesh['ctx'=16,'exp'=16] {'exp'}, dimensions={0} | all-to-all | bytes 1638400 | tf_op jit(solution)/shard_map/all_to_all | solution.py:122
  803.4 1.6 fusion.2
  (24 shorter events, 0.1 us)
Async XLA Ops:
  6.5 560.8 %copy-start = (bf16[1,256,5120]{2,1,0:T(8,128)(2,1)S(1)}, bf16[1,256,5120]{2,1,0:T(8,128)(2,1)}, u32[]{:S(2)}) copy-start(bf16[1,256,5120]{2,1,0:T(8,128)(2,1)} %param.23) | copy-start | bytes 7864324
  6.5 60.7 %all-gather.10.cloned.1.call-start = ((), (), s32[]{:S(2)}) async-start(), calls=%async_computation.8 | async-start | bytes 1114112 | tf_op jit(solution)/shard_map/all_gather | solution.py:40
  7.3 113.8 %all-gather.12.cloned.1.call-start = ((), (), s32[]{:S(2)}) async-start(), calls=%async_computation.9 | async-start | bytes 1114112 | tf_op jit(solution)/shard_map/all_gather | solution.py:41
  8.0 194.9 %all-gather.14.cloned.1.call-start = ((), (), s32[]{:S(2)}) async-start(), calls=%async_computation.10 | async-start | bytes 2785280 | tf_op jit(solution)/shard_map/all_gather | solution.py:70
  125.7 1.6 copy-start.4
  132.5 74.4 %all-to-all-start = ((bf16[64,16,160]{2,0,1:T(8,128)(2,1)}), bf16[64,16,160]{2,0,1:T(8,128)(2,1)S(1)}, u32[]{:S(2)}, u32[]{:S(2)}) async-start(bf16[64,16,160]{2,0,1:T(8,128)(2,1)} %copy.40), calls=%async_computation | async-start | bytes 1048576 | tf_op jit(solution)/shard_map/all_to_all | solution.py:71
  136.8 237.9 %reduce-scatter.3.cloned.1.call-start = ((), (), s32[]{:S(2)}) async-start(), calls=%async_computation.5 | async-start | bytes 11141120 | tf_op jit(solution)/shard_map/reduce_scatter | solution.py:79
  213.9 0.7 copy-start.6
  213.9 0.9 copy-start.5
  213.9 160.7 %copy-start.1 = (bf16[1,64,5120]{2,1,0:T(8,128)(2,1)S(1)}, bf16[1,64,5120]{2,1,0:T(8,128)(2,1)}, u32[]{:S(2)}) copy-start(bf16[1,64,5120]{2,1,0:T(8,128)(2,1)} %param.16) | copy-start | bytes 1966084
  213.9 162.2 %copy-start.7 = (bf16[5120,16]{0,1:T(8,128)(2,1)S(1)}, bf16[5120,16]{0,1:T(8,128)(2,1)}, u32[]{:S(2)}) copy-start(bf16[5120,16]{0,1:T(8,128)(2,1)} %param.19) | copy-start | bytes 491524
  214.0 343.2 %all-gather.8.cloned.1.call-start = ((), (), s32[]{:S(2)}) async-start(), calls=%async_computation.6 | async-start | bytes 13926400 | tf_op jit(solution)/shard_map/all_gather | solution.py:111
  374.7 3.0 copy-start.2
  417.5 346.3 %reduce-scatter.5.cloned.1.call-start = ((), (), s32[]{:S(2)}) async-start(), calls=%async_computation.7 | async-start | bytes 13926400 | tf_op jit(solution)/shard_map/reduce_scatter | solution.py:115
  766.0 37.4 %copy-start.3 = (bf16[64,5120]{1,0:T(8,128)(2,1)S(1)}, bf16[64,5120]{1,0:T(8,128)(2,1)}, u32[]{:S(2)}) copy-start(bf16[64,5120]{1,0:T(8,128)(2,1)} %reduce-scatter.3.cloned.1.call-done) | copy-start | bytes 1966084
Sparse Core Ops, SparseCore 0:
  10.0 57.1 all-gather.9
  69.9 51.0 all-gather.11
  122.9 80.0 all-gather.13
  214.1 160.5 reduce-scatter.2
  417.6 139.5 all-gather.7
  587.8 175.8 reduce-scatter.4
where the time goes:
time: 813 us; the launch traced here: 812 us
  waiting for transfers between devices  651 us (80%)
  blocking collectives  74 us (9%)
  matrix products  45.1 us (6%)
  local copies, waits for them, and re-layouts  19.1 us (2%)
  between operations  13.6 us (2%)
    reduce_scatter x1, waiting for transfers between devices, local(): lax.psum_scatter(jnp.dot(inner, down_local, preferred_element_type=jnp.fl...  176 us
    reduce_scatter x1, waiting for transfers between devices, local(): lax.psum_scatter(jnp.dot(feature_rows, proj_rows, preferred_element_type=...  160 us
    all_gather x1, waiting for transfers between devices, local(): piece = lax.all_gather(arrived_rows, 'ctx', axis=0, tiled=True)  139 us
    all_gather x1, waiting for transfers between devices, local(): proj_rows = lax.all_gather(out_weight, 'exp', axis=0, tiled=True)  66.1 us
    all_gather x1, waiting for transfers between devices, local(): key_piece = lax.all_gather(keys[0], 'ctx', axis=0, tiled=True)  56 us
    all_gather x1, waiting for transfers between devices, local(): value_piece = lax.all_gather(values[0], 'ctx', axis=0, tiled=True)  51.5 us
    all_to_all x1, blocking collectives, local(): lax.all_to_all(expert_out, 'exp', split_axis=0, concat_axis=0, tiled=True)  37.4 us
    all_to_all x1, blocking collectives, local(): lax.all_to_all(outgoing, 'exp', split_axis=0, concat_axis=0, tiled=True)  36.6 us
  transfers between devices with their start and end apart: 7, of which 6 were waited for; matrix products, arithmetic and copies ran while one was open for 3% of the time, Pallas kernels for 0%

commit v1 on v0

--- a/solution.py
+++ b/solution.py
@@ -37,7 +37,9 @@
     heads_of_query = queries[0].reshape(tok_rows, kv_heads, head_groups, HEAD_SIZE)
     scale = 1.0 / math.sqrt(HEAD_SIZE)
     best = jnp.full((kv_heads, head_groups, tok_rows), -1e30, jnp.float32)
-    key_piece = lax.all_gather(keys[0], "ctx", axis=0, tiled=True)
+    key_piece = jnp.concatenate(
+        lax.all_to_all(jnp.stack([keys[0]] * lax.axis_size("ctx")), "ctx", 0, 0), axis=0
+    )
     value_piece = lax.all_gather(values[0], "ctx", axis=0, tiled=True)
     count = key_piece.shape[0]
     heads_of_key = key_piece.reshape(count, kv_heads, HEAD_SIZE)

time: 813 us -> 762 us (0.937)
  waiting for transfers between devices: 651 us -> 590 us
  starting transfers between devices: 4.61 us -> 14.8 us
    all_gather x1 -> x0, waiting for transfers between devices: 56 us -> none  [local(): key_piece = lax.all_gather(keys[0], 'ctx', axis=0, tiled=True)]
    all_to_all x0 -> x1, starting transfers between devices: none -> 10.2 us  [local(): lax.all_to_all(jnp.stack([keys[0]] * lax.axis_size('ctx')), 'ctx', 0, 0)]
  transfers between devices with their start and end apart: 7 -> 7, of which waited for: 6 -> 5; matrix products, arithmetic and copies ran while one was open for 3% -> 3% of each run, Pallas kernels for 0% -> 0%
where the time goes in v1:
time: 762 us; the launch traced here: 761 us
  waiting for transfers between devices  590 us (77%)
  blocking collectives  74 us (10%)
  matrix products  45.2 us (6%)
  local copies, waits for them, and re-layouts  20.1 us (3%)
  starting transfers between devices  14.8 us (2%)
  between operations  13.3 us (2%)
    reduce_scatter x1, waiting for transfers between devices, local(): lax.psum_scatter(jnp.dot(inner, down_local, preferred_element_type=jnp.fl...  176 us
    reduce_scatter x1, waiting for transfers between devices, local(): lax.psum_scatter(jnp.dot(feature_rows, proj_rows, preferred_element_type=...  161 us
    all_gather x1, waiting for transfers between devices, local(): piece = lax.all_gather(arrived_rows, 'ctx', axis=0, tiled=True)  139 us
    all_gather x1, waiting for transfers between devices, local(): proj_rows = lax.all_gather(out_weight, 'exp', axis=0, tiled=True)  62.1 us
    all_gather x1, waiting for transfers between devices, local(): value_piece = lax.all_gather(values[0], 'ctx', axis=0, tiled=True)  50.4 us
    all_to_all x1, blocking collectives, local(): lax.all_to_all(expert_out, 'exp', split_axis=0, concat_axis=0, tiled=True)  37.4 us
    all_to_all x1, blocking collectives, local(): lax.all_to_all(outgoing, 'exp', split_axis=0, concat_axis=0, tiled=True)  36.6 us
    dot_general x1, matrix products, local(): jnp.dot(inner, down_local, preferred_element_type=jnp.float32)  20.4 us
  transfers between devices with their start and end apart: 7, of which 5 were waited for; matrix products, arithmetic and copies ran while one was open for 3% of the time, Pallas kernels for 0%

profile of v1, /device:TPU:32, one launch (start us, length us, event | category | flops | bytes accessed | tf_op | source)
XLA Modules:
  0.0 761.3 jit_solution(10617108604219120452)
XLA Ops:
  6.5 0.7 all-gather.8.cloned.1.call-update
  7.3 2.0 stack.3
  9.3 10.2 %all-to-all-start = ((bf16[16,64,512]{2,1,0:T(8,128)(2,1)}), bf16[16,64,512]{2,1,0:T(8,128)(2,1)}, u32[]{:S(2)}, u32[]{:S(2)}) async-start(bf16[16,64,512]{2,1,0:T(8,128)(2,1)} %stack.3), calls=%async_computation | async-start | bytes 2097152 | tf_op jit(solution)/shard_map/all_to_all | solution.py:41
  19.5 0.0 all-gather.10.cloned.1.call-start
  19.5 0.7 all-gather.10.cloned.1.call-update
  20.2 0.4 reshape_squeeze.3
  20.6 0.0 copy-done.9
  20.6 0.2 reduce-window.8
  20.8 0.1 convert_reduce_fusion
  20.9 0.1 convert_reduce_fusion.1
  21.0 0.1 fusion.50
  21.1 50.4 %all-gather.8.cloned.1.call-done = bf16[1,1024,512]{2,1,0:T(8,128)(2,1)} async-done(((bf16[1,64,512]{2,1,0:T(8,128)(2,1)}), bf16[1,1024,512]{2,1,0:T(8,128)(2,1)}) %all-gather.8.cloned.1.call-update) | async-done | bytes 1048592 | tf_op jit(solution)/shard_map/all_gather | solution.py:43
  71.6 2.3 copy.34
  73.8 0.0 all-to-all-done
  73.8 2.2 reshape_reshape.3
  76.0 2.5 fusion.3
  78.5 1.6 fusion.4
  80.1 1.5 fusion.34
  81.6 0.2 copy.36
  81.9 1.4 convert_element_type.64
  83.3 2.0 copy.37
  85.3 4.2 all-to-all-start.1
  89.5 0.0 reduce-scatter.3.cloned.1.call-start
  89.6 62.1 %all-gather.10.cloned.1.call-done = bf16[16,10,5120]{2,1,0:T(8,128)(2,1)} async-done(((bf16[1,10,5120]{2,1,0:T(8,128)(2,1)}), bf16[16,10,5120]{2,1,0:T(8,128)(2,1)}) %all-gather.10.cloned.1.call-update) | async-done | bytes 1638416 | tf_op jit(solution)/shard_map/all_gather | solution.py:72
  151.7 4.0 reshape.128
  155.7 0.0 all-to-all-done.1
  155.7 6.9 convolution_convert_fusion.1
  162.7 0.0 reduce-scatter.3.cloned.1.call-update
  162.7 0.0 all-gather.6.cloned.1.call-start
  162.7 0.6 copy-done.7
  163.3 0.2 fusion.28
  163.6 160.8 %reduce-scatter.3.cloned.1.call-done = bf16[64,5120]{1,0:T(8,128)(2,1)} async-done(((bf16[1024,5120]{1,0:T(8,128)(2,1)}), bf16[64,5120]{1,0:T(8,128)(2,1)}) %reduce-scatter.3.cloned.1.call-update) | async-done | bytes 655376 | tf_op jit(solution)/shard_map/reduce_scatter | solution.py:81
  324.4 1.5 multiply_reduce_fusion
  325.9 1.5 fusion.27
  327.4 0.5 convolution_convert_fusion.2
  327.8 0.5 copy.39
  328.3 36.6 %all_to_all.30 = bf16[16,5,5120]{2,1,0:T(8,128)(2,1)} all-to-all(bf16[16,5,5120]{2,1,0:T(8,128)(2,1)S(1)} %copy.39), channel_id=1, replica_groups=mesh['ctx'=16,'exp'=16] {'exp'}, dimensions={0} | all-to-all | bytes 1638400 | tf_op jit(solution)/shard_map/all_to_all | solution.py:108
  365.0 2.2 reshape.122
  367.2 0.0 all-gather.6.cloned.1.call-update
  367.2 0.2 reduce-scatter.5.cloned.1.call-start
  367.4 139.5 %all-gather.6.cloned.1.call-done = bf16[1280,5120]{1,0:T(8,128)(2,1)} async-done(((bf16[80,5120]{1,0:T(8,128)(2,1)}), bf16[1280,5120]{1,0:T(8,128)(2,1)}) %all-gather.6.cloned.1.call-update) | async-done | bytes 13107216 | tf_op jit(solution)/shard_map/all_gather | solution.py:113
  506.9 10.1 %fusion.8 = f32[1280,256]{1,0:T(8,128)} fusion(bf16[1280,5120]{1,0:T(8,128)(2,1)} %all-gather.6.cloned.1.call-done, bf16[1,5120,256]{2,1,0:T(8,128)(2,1)} %param.21), kind=kOutput, calls=%fused_computation.15 | convolution fusion | flops 3355443200 | bytes 17039360 | tf_op jit(solution)/shard_map/dot_general | solution.py:114
  517.0 20.4 %convolution_convert_fusion = bf16[1280,5120]{1,0:T(8,128)(2,1)} fusion(bf16[1,256,5120]{2,1,0:T(8,128)(2,1)S(1)} %copy-done, bf16[1280,5120]{1,0:T(8,128)(2,1)} %all-gather.6.cloned.1.call-done, bf16[1,5120,256]{2,1,0:T(8,128)(2,1)} %param.22, f32[1280,256]{1,0:T(8,128)} %fusion.8), kind=kOutput, calls=%fused_computation | convolution fusion | flops 6719406080 | bytes 32768000 | tf_op jit(solution)/shard_map/dot_general | solution.py:118
  537.4 0.0 reduce-scatter.5.cloned.1.call-update
  537.4 176.1 %reduce-scatter.5.cloned.1.call-done = bf16[80,5120]{1,0:T(8,128)(2,1)} async-done(((bf16[1280,5120]{1,0:T(8,128)(2,1)}), bf16[80,5120]{1,0:T(8,128)(2,1)}) %reduce-scatter.5.cloned.1.call-update) | async-done | bytes 819216 | tf_op jit(solution)/shard_map/reduce_scatter | solution.py:117
  713.5 2.3 reshape.123
  715.7 37.4 %all_to_all.31 = bf16[16,5,5120]{2,1,0:T(8,128)(2,1)S(1)} all-to-all(bf16[16,5,5120]{2,1,0:T(8,128)(2,1)} %reshape.123), channel_id=1, replica_groups=mesh['ctx'=16,'exp'=16] {'exp'}, dimensions={0} | all-to-all | bytes 1638400 | tf_op jit(solution)/shard_map/all_to_all | solution.py:124
  753.1 1.6 fusion.2
  (28 shorter events, 0.1 us)
Async XLA Ops:
  6.5 510.5 %copy-start = (bf16[1,256,5120]{2,1,0:T(8,128)(2,1)S(1)}, bf16[1,256,5120]{2,1,0:T(8,128)(2,1)}, u32[]{:S(2)}) copy-start(bf16[1,256,5120]{2,1,0:T(8,128)(2,1)} %param.23) | copy-start | bytes 7864324
  6.5 13.7 %copy-start.5 = (bf16[1,64,2560]{2,1,0:T(8,128)(2,1)S(1)}, bf16[1,64,2560]{2,1,0:T(8,128)(2,1)}, u32[]{:S(2)}) copy-start(bf16[1,64,2560]{2,1,0:T(8,128)(2,1)} %param.12) | copy-start | bytes 983044
  6.5 14.1 %copy-start.9 = (s32[1,4]{1,0:T(1,128)S(1)}, s32[1,4]{1,0:T(1,128)}, u32[]{:S(2)}) copy-start(s32[1,4]{1,0:T(1,128)} %param.15) | copy-start | bytes 52
  6.5 65.0 %all-gather.8.cloned.1.call-start = ((), (), s32[]{:S(2)}) async-start(), calls=%async_computation.9 | async-start | bytes 1114112 | tf_op jit(solution)/shard_map/all_gather | solution.py:43
  9.3 64.6 %all-to-all-start = ((bf16[16,64,512]{2,1,0:T(8,128)(2,1)}), bf16[16,64,512]{2,1,0:T(8,128)(2,1)}, u32[]{:S(2)}, u32[]{:S(2)}) async-start(bf16[16,64,512]{2,1,0:T(8,128)(2,1)} %stack.3), calls=%async_computation | async-start | bytes 2097152 | tf_op jit(solution)/shard_map/all_to_all | solution.py:41
  19.5 132.2 %all-gather.10.cloned.1.call-start = ((), (), s32[]{:S(2)}) async-start(), calls=%async_computation.10 | async-start | bytes 2785280 | tf_op jit(solution)/shard_map/all_gather | solution.py:72
  78.5 1.6 copy-start.4
  85.3 70.4 %all-to-all-start.1 = ((bf16[64,16,160]{2,0,1:T(8,128)(2,1)}), bf16[64,16,160]{2,0,1:T(8,128)(2,1)S(1)}, u32[]{:S(2)}, u32[]{:S(2)}) async-start(bf16[64,16,160]{2,0,1:T(8,128)(2,1)} %copy.37), calls=%async_computation.1 | async-start | bytes 1048576 | tf_op jit(solution)/shard_map/all_to_all | solution.py:73
  89.5 234.8 %reduce-scatter.3.cloned.1.call-start = ((), (), s32[]{:S(2)}) async-start(), calls=%async_computation.6 | async-start | bytes 11141120 | tf_op jit(solution)/shard_map/reduce_scatter | solution.py:81
  162.6 0.7 copy-start.7
  162.6 0.9 copy-start.6
  162.6 161.7 %copy-start.1 = (bf16[1,64,5120]{2,1,0:T(8,128)(2,1)S(1)}, bf16[1,64,5120]{2,1,0:T(8,128)(2,1)}, u32[]{:S(2)}) copy-start(bf16[1,64,5120]{2,1,0:T(8,128)(2,1)} %param.16) | copy-start | bytes 1966084
  162.7 163.2 %copy-start.8 = (bf16[5120,16]{0,1:T(8,128)(2,1)S(1)}, bf16[5120,16]{0,1:T(8,128)(2,1)}, u32[]{:S(2)}) copy-start(bf16[5120,16]{0,1:T(8,128)(2,1)} %param.19) | copy-start | bytes 491524
  162.7 344.2 %all-gather.6.cloned.1.call-start = ((), (), s32[]{:S(2)}) async-start(), calls=%async_computation.7 | async-start | bytes 13926400 | tf_op jit(solution)/shard_map/all_gather | solution.py:113
  324.4 3.0 copy-start.2
  367.2 346.3 %reduce-scatter.5.cloned.1.call-start = ((), (), s32[]{:S(2)}) async-start(), calls=%async_computation.8 | async-start | bytes 13926400 | tf_op jit(solution)/shard_map/reduce_scatter | solution.py:117
  715.7 37.4 %copy-start.3 = (bf16[64,5120]{1,0:T(8,128)(2,1)S(1)}, bf16[64,5120]{1,0:T(8,128)(2,1)}, u32[]{:S(2)}) copy-start(bf16[64,5120]{1,0:T(8,128)(2,1)} %reduce-scatter.3.cloned.1.call-done) | copy-start | bytes 1966084
Sparse Core Ops, SparseCore 0:
  10.0 61.4 all-gather.7
  73.3 78.2 all-gather.9
  162.8 161.5 reduce-scatter.2
  367.3 139.5 all-gather.5
  537.5 175.8 reduce-scatter.4
